TPU v7x, 32 devices: a whole 2x2x4 slice. The times are simulated.
32 devices in a mesh: wl: 2 (over y), row: 16 (over z, x, core).
Axes of the slice: x: 2, y: 2, z: 4, core: 2. Of those that a mesh axis runs over, the one named last changes fastest.
Arguments:
- scenes: float32 [2, 4096, 4096], P(None, 'row'), may hold values from -6 to 6
- optics: bfloat16 [4, 2, 4096, 4096], P('wl', None, 'row'), may hold values from -4 to 4
- weights: float32 [4, 2], replicated, may hold values from 0.1 to 2
Outputs:
- blurred: float32 [2, 4096, 4096], P(None, 'row', 'wl')
All inputs are finite; a program needn't handle non-finite values.
Results may differ from a plain program's by a relative error of at most 0.0003.
Values may be sent and summed in bfloat16 or wider, within the bound.
No kernel may reach another device: no remote copies, remote signals or barrier semaphores. Data moves between devices by JAX's collectives and lax.ppermute only.
A program may use at most 128 MiB of HBM per device.

v0:
```python
import math
import jax
import jax.numpy as jnp
from jax import lax
from jax.sharding import PartitionSpec as P

PRECISE = lax.Precision.HIGHEST
NARROW = 32


def phase(left_ids, right_ids, modulus, orient):
    turns = (left_ids * right_ids % modulus).astype(jnp.float32)
    angles = turns * (orient * 2.0 * math.pi / modulus)
    return (jnp.cos(angles), jnp.sin(angles))


def ids(count):
    return jnp.arange(count, dtype=jnp.int32)


def cblock(cos_part, sin_part):
    return jnp.stack([jnp.stack([cos_part, -sin_part]), jnp.stack([sin_part, cos_part])])


def small_tables(out_count, in_count, modulus, orients):
    tables = []
    for orient in orients:
        cos_part, sin_part = phase(ids(out_count)[:, None], ids(in_count)[None, :], modulus, orient)
        tables.append(cblock(cos_part, sin_part))
    return jnp.stack(tables)


def twist(values, axis_e, cos_part, sin_part):
    real = jnp.take(values, 0, axis=axis_e)
    imag = jnp.take(values, 1, axis=axis_e)
    return jnp.stack([real * cos_part - imag * sin_part, real * sin_part + imag * cos_part], axis_e)


def canon_to_groups(canon, group_count):
    mcount, span_c = (canon.shape[0], canon.shape[-1] // 2)
    mid = canon.shape[1:-1]
    if group_count == mcount:
        return canon
    span = mcount * span_c // group_count
    flat = jnp.moveaxis(canon.reshape((mcount,) + mid + (2, span_c)), 0, -2)
    flat = flat.reshape(mid + (2, group_count, span))
    return jnp.moveaxis(flat, -2, 0).reshape((group_count,) + mid + (2 * span,))


def groups_to_canon(grouped, mcount, axis_g):
    group_count = grouped.shape[axis_g]
    if group_count == mcount:
        return grouped
    moved = jnp.moveaxis(grouped, axis_g, 0)
    mid = moved.shape[1:-1]
    span = moved.shape[-1] // 2
    span_c = group_count * span // mcount
    flat = jnp.moveaxis(moved.reshape((group_count,) + mid + (2, span)), 0, -2)
    flat = flat.reshape(mid + (2, mcount, span_c))
    canon = jnp.moveaxis(flat, -2, 0).reshape((mcount,) + mid + (2 * span_c,))
    return jnp.moveaxis(canon, 0, axis_g)


def forward_rows(scenes):
    rows_here, length = (scenes.shape[1], scenes.shape[2])
    across = length // NARROW
    half_k = across // 2
    grid = scenes.reshape((2, rows_here, NARROW, across))
    first_tab = jnp.transpose(small_tables(NARROW, NARROW, NARROW, (-1.0, 1.0)), (0, 3, 1, 2, 4))
    first = jnp.einsum("oaedb,drbn->oaern", first_tab, grid, precision=PRECISE)
    tw_cos, tw_sin = ([], [])
    for orient in (-1.0, 1.0):
        cos_part, sin_part = phase(ids(NARROW)[:, None], ids(across)[None, :], length, orient)
        tw_cos.append(cos_part)
        tw_sin.append(sin_part)
    tw_cos = jnp.stack(tw_cos)[:, :, None, :]
    tw_sin = jnp.stack(tw_sin)[:, :, None, :]
    turned = twist(first, 2, tw_cos, tw_sin)
    second_tab = jnp.transpose(small_tables(half_k, across, across, (-1.0, 1.0)), (0, 2, 4, 1, 3))
    second = jnp.einsum("oaern,oenfk->oarfk", turned, second_tab, precision=PRECISE)
    signs = 1.0 - 2.0 * (ids(across) % 2).astype(jnp.float32)
    nyquist = jnp.einsum("ern,n->er", first[0, 0], signs, precision=PRECISE)
    per_block = across // NARROW
    mcount = half_k // per_block
    blocks = second.reshape((2, NARROW, rows_here, 2, mcount, per_block))
    canon = jnp.transpose(blocks, (4, 3, 2, 0, 5, 1)).reshape((mcount, 2, rows_here, 2 * across))
    canon = canon.at[0, :, :, across].set(nyquist)
    return canon


def forward_cols(columns):
    length, width = (columns.shape[1], columns.shape[2])
    across = length // NARROW
    grid = columns.reshape((2, NARROW, across, width))
    first_tab = jnp.transpose(small_tables(NARROW, NARROW, NARROW, (-1.0, 1.0)), (0, 3, 1, 2, 4))
    first = jnp.einsum("oafeb,ebnj->oafnj", first_tab, grid, precision=PRECISE)
    tw_cos, tw_sin = ([], [])
    for orient in (-1.0, 1.0):
        cos_part, sin_part = phase(ids(NARROW)[:, None], ids(across)[None, :], length, orient)
        tw_cos.append(cos_part)
        tw_sin.append(sin_part)
    tw_cos = jnp.stack(tw_cos)[:, :, :, None]
    tw_sin = jnp.stack(tw_sin)[:, :, :, None]
    turned = twist(first, 2, tw_cos, tw_sin)
    second_tab = small_tables(across, across, across, (-1.0, 1.0))
    second = jnp.einsum("ofekn,oaenj->ofkaj", second_tab, turned, precision=PRECISE)
    return second.reshape((2, 2, length, width))


def inverse_cols_half(combined, group_count, half_index, part=0, parts=1):
    length, width = (combined.shape[1], combined.shape[2])
    across = length // NARROW
    grid = combined.reshape((2, NARROW, across, width))
    first_tab = jnp.transpose(small_tables(NARROW, NARROW, NARROW, (1.0,))[0], (2, 0, 1, 3))
    first = jnp.einsum("afeb,ebnj->afnj", first_tab, grid, precision=PRECISE)
    cos_part, sin_part = phase(ids(NARROW)[:, None], ids(across)[None, :], length, 1.0)
    turned = twist(first, 1, cos_part[:, :, None], sin_part[:, :, None])
    per_group = across // group_count
    per_half = per_group // 2
    per_part = per_half // parts
    k_ids = ids(per_part)[None, :] + part * per_part
    k_ids = ids(group_count)[:, None] * per_group + half_index * per_half + k_ids
    cos_k, sin_k = phase(k_ids.reshape((-1, 1)), ids(across)[None, :], across, 1.0)
    second_tab = jnp.transpose(cblock(cos_k, sin_k), (0, 2, 1, 3))
    second = jnp.einsum("fken,aenj->fkaj", second_tab, turned, precision=PRECISE)
    return second.reshape((2, group_count, per_part * NARROW, width))


def inverse_cols(combined):
    length, width = (combined.shape[1], combined.shape[2])
    across = length // NARROW
    grid = combined.reshape((2, NARROW, across, width))
    first_tab = jnp.transpose(small_tables(NARROW, NARROW, NARROW, (1.0,))[0], (2, 0, 1, 3))
    first = jnp.einsum("afeb,ebnj->afnj", first_tab, grid, precision=PRECISE)
    cos_part, sin_part = phase(ids(NARROW)[:, None], ids(across)[None, :], length, 1.0)
    turned = twist(first, 1, cos_part[:, :, None], sin_part[:, :, None])
    second_tab = jnp.transpose(small_tables(across, across, across, (1.0,))[0], (0, 2, 1, 3))
    second = jnp.einsum("fken,aenj->fkaj", second_tab, turned, precision=PRECISE)
    return second.reshape((2, length, width))


def inverse_rows(canon, length, scale, k_count=None, k_start=0):
    mcount, rows_here, width = (canon.shape[1], canon.shape[2], canon.shape[3])
    across = width // 2
    k_count = across if k_count is None else k_count
    first_tab = jnp.transpose(small_tables(NARROW, mcount, NARROW, (1.0, -1.0)), (0, 3, 1, 2, 4))
    first = jnp.einsum("oafem,emRj->oafRj", first_tab, canon, precision=PRECISE)
    lower = first[0, :, :, :, :across]
    upper = first[1, :, :, :, across:]
    flip_gain = -2.0 * (ids(NARROW) % 2).astype(jnp.float32)
    fix = flip_gain[:, None, None] * canon[:, 0, :, across][None]
    lane0 = (ids(across) == 0)[None, None, None, :]
    upper = jnp.where(lane0, upper + fix[..., None], upper)
    cos_up, sin_up = phase(ids(NARROW)[:, None], ids(across)[None, :], length, 1.0)
    cos_dn, sin_dn = phase(ids(NARROW)[:, None], ids(across)[None, :], length, -1.0)
    lower = twist(lower, 1, cos_up[:, None, :], sin_up[:, None, :])
    upper = twist(upper, 1, cos_dn[:, None, :], sin_dn[:, None, :])
    tabs = []
    for orient in (1.0, -1.0):
        k_ids = ids(k_count)[:, None] + k_start
        cos_part, sin_part = phase(k_ids, ids(across)[None, :], across, orient)
        tabs.append(cblock(cos_part, sin_part))
    tabs = jnp.transpose(jnp.stack(tabs) * scale, (0, 2, 4, 1, 3))
    out = jnp.einsum("aeRu,eufk->aRfk", lower, tabs[0], precision=PRECISE)
    out = out + jnp.einsum("aeRu,eufk->aRfk", upper, tabs[1], precision=PRECISE)
    return jnp.transpose(out, (2, 1, 3, 0)).reshape((2, rows_here, k_count * NARROW))


def pair_optics(optics):
    length = optics.shape[-1]
    across = length // NARROW
    half = length // 2
    mcount = half // across
    block = [lax.slice_in_dim(optics, across * i, across * (i + 1), axis=3) for i in range(NARROW)]
    windows = []
    for m in range(mcount):
        second = block[half // across if m == 0 else NARROW - m]
        windows.append(jnp.concatenate([block[NARROW - 1 - m], second], -1))
    windows = jnp.stack(windows)
    src = ids(2 * across)[:, None]
    dst = ids(across)[None, :]
    picker = jnp.logical_or(
        jnp.logical_and(src == across - dst, dst > 0), jnp.logical_and(src == across, dst == 0)
    ).astype(optics.dtype)
    mirrored = jnp.einsum("mwcpv,vu->mwcpu", windows, picker, preferred_element_type=jnp.float32)
    lower = jnp.stack(block[:mcount])
    return jnp.concatenate([lower, mirrored.astype(optics.dtype)], -1)


def local(scenes, optics, weights):
    row_count = lax.axis_size("row")
    length = scenes.shape[2]
    across = length // NARROW
    norm_factor = 1.0 / (float(length) * float(length))
    wl_index = lax.axis_index("wl")
    local_waves = optics.shape[0]
    weight_rows = lax.dynamic_slice_in_dim(weights, wl_index * local_waves, local_waves, 0)
    first_row = lax.axis_index("row") == 0
    wl_count = lax.axis_size("wl")
    rows_here = scenes.shape[1]
    own_rows = rows_here // wl_count
    if wl_count == 2 and own_rows * wl_count == rows_here:
        mine = lax.dynamic_slice_in_dim(scenes, wl_index * own_rows, own_rows, 1)
        canon = forward_rows(mine)
        mcount = canon.shape[0]
        sent = canon_to_groups(canon, row_count)
        got = lax.all_to_all(sent, "row", split_axis=0, concat_axis=2, tiled=True)[0]
        other = lax.ppermute(got, "wl", perm=[(0, 1), (1, 0)])
        got = got.reshape((2, row_count, own_rows, got.shape[-1]))
        other = other.reshape(got.shape)
        first_half = jnp.where(wl_index == 0, got, other)
        second_half = jnp.where(wl_index == 0, other, got)
        got = jnp.stack([first_half, second_half], 2).reshape((2, length, got.shape[-1]))
    else:
        canon = forward_rows(scenes)
        mcount = canon.shape[0]
        sent = canon_to_groups(canon, row_count)
        got = lax.all_to_all(sent, "row", split_axis=0, concat_axis=2, tiled=True)[0]
    spec = forward_cols(got)
    optic_canon = pair_optics(optics)
    optic_sent = canon_to_groups(optic_canon, row_count)
    optic_got = lax.all_to_all(optic_sent, "row", split_axis=0, concat_axis=3, tiled=True)[0]
    width = spec.shape[-1]
    span = width // 2
    lane_ids = ids(width)
    itself = jnp.logical_and(first_row, lane_ids % span == 0)
    direct = spec[0]
    flipped = spec[1]
    swapped = jnp.concatenate([flipped[..., span:], flipped[..., :span]], -1)
    partner = jnp.where(itself, flipped, swapped)
    mirror_real = partner[0]
    mirror_imag = -partner[1]
    even_real = 0.5 * (direct[0] + mirror_real)
    even_imag = 0.5 * (direct[1] + mirror_imag)
    odd_real = 0.5 * (direct[0] - mirror_real)
    odd_imag = 0.5 * (direct[1] - mirror_imag)
    combined_real = jnp.zeros_like(even_real)
    combined_imag = jnp.zeros_like(even_imag)
    for colour in range(local_waves):
        mixed_real = weight_rows[colour, 0] * even_real + weight_rows[colour, 1] * odd_real
        mixed_imag = weight_rows[colour, 0] * even_imag + weight_rows[colour, 1] * odd_imag
        resp_real = optic_got[colour, 0].astype(jnp.float32)
        resp_imag = optic_got[colour, 1].astype(jnp.float32)
        combined_real = combined_real + resp_real * mixed_real - resp_imag * mixed_imag
        combined_imag = combined_imag + resp_real * mixed_imag + resp_imag * mixed_real
    stacked = jnp.stack([combined_real, combined_imag])
    back = inverse_cols(stacked)
    if wl_count != 2 or own_rows * wl_count != rows_here:
        back = back.reshape((2, row_count, rows_here, width))
        returned = lax.all_to_all(back, "row", split_axis=1, concat_axis=1, tiled=True)
        returned = groups_to_canon(returned, mcount, 1)
        result_image = inverse_rows(returned, length, norm_factor)
        return lax.psum_scatter(result_image, "wl", scatter_dimension=2, tiled=True)
    per_group = across // row_count
    if per_group % 2 == 0 and per_group * row_count == across:
        parts = 4 if per_group % 8 == 0 else 1
        incoming = []
        for part in range(parts):
            given = inverse_cols_half(stacked, row_count, 1 - wl_index, part, parts)
            incoming.append(lax.ppermute(given, "wl", perm=[(0, 1), (1, 0)]))
        incoming = jnp.concatenate(incoming, 2)
        kept = inverse_cols_half(stacked, row_count, wl_index)
    else:
        back = back.reshape((2, row_count, 2, own_rows, width))
        kept = lax.dynamic_index_in_dim(back, wl_index, 2, keepdims=False)
        given = lax.dynamic_index_in_dim(back, 1 - wl_index, 2, keepdims=False)
        incoming = lax.ppermute(given, "wl", perm=[(0, 1), (1, 0)])
    summed = kept + incoming
    returned = lax.all_to_all(summed, "row", split_axis=1, concat_axis=1, tiled=True)
    returned = groups_to_canon(returned, mcount, 1)
    k_half = across // 2
    theirs = inverse_rows(returned, length, norm_factor, k_half, (1 - wl_index) * k_half)
    taken = lax.ppermute(theirs, "wl", perm=[(0, 1), (1, 0)])
    mine = inverse_rows(returned, length, norm_factor, k_half, wl_index * k_half)
    upper = jnp.where(wl_index == 0, mine, taken)
    lower = jnp.where(wl_index == 0, taken, mine)
    return jnp.concatenate([upper, lower], 1)


def solution(mesh):
    in_specs = (P(None, "row", None), P("wl", None, "row", None), P())
    out_specs = P(None, "row", "wl")
    return jax.shard_map(local, mesh=mesh, in_specs=in_specs, out_specs=out_specs, check_vma=False)
```

profile of v0, /device:TPU:10, one launch (start us, length us, event | category | flops | bytes accessed | tf_op | source)
XLA Modules:
  0.0 713.1 jit_solution(16438513354789603543)
XLA Ops:
  5.1 6.8 fusion.46
  15.1 13.9 %fusion.17 = f32[2,32,128,2,64,1]{2,4,5,3,1,0:T(8,128)S(1)} fusion(f32[2,32,2,128,128,1]{4,1,3,0,2,5:T(8,128)S(1)} %maximum_bitcast_fusion.1, f32[1,2,2,64,128]{4,3,2,1,0:T(8,128)S(1)} %maximum_bitcast_fusion.22, f32[1,2,2,64,128]{4,3,2,1,0:T(8,128)S(1)} %maximum_bitcast_fusion.21), kind=kOutput, calls=%fused_computation.26 | convolution fusion | flops 3221291008 | bytes 12845056 | tf_op jit(solution)/shard_map/oaern,oenfk->oarfk/dot_general | solution.py:80
  39.4 6.2 all-to-all-start.1
  98.0 7.8 %pad_maximum_fusion = bf16[16,2,2,256,256]{3,4,2,1,0:T(8,128)(2,1)} fusion(bf16[16,2,2,256,128]{3,4,2,1,0:T(8,128)(2,1)} %convolution_convert_fusion, bf16[16,2,2,256,128]{3,4,2,1,0:T(8,128)(2,1)} %bitcast_dynamic-update-slice_fusion.15), kind=kLoop, calls=%fused_computation.5 | loop fusion | flops 16777216 | bytes 16777216 | tf_op jit(solution)/shard_map/concatenate | solution.py:187
  105.9 32.1 %all-to-all-done.1 = f32[16,2,128,256]{2,3,1,0:T(8,128)} async-done(((f32[16,2,128,256]{2,3,1,0:T(8,128)}), f32[16,2,128,256]{2,3,1,0:T(8,128)}, u32[]{:S(2)}, u32[]{:S(2)}) %all-to-all-start.1) | async-done | bytes 4194336 | tf_op jit(solution)/shard_map/all_to_all | solution.py:207
  160.9 80.8 %collective-permute-done = f32[2,2048,256]{2,1,0:T(8,128)} collective-permute-done((f32[2,2048,256]{2,1,0:T(8,128)}, f32[2,2048,256]{2,1,0:T(8,128)}, u32[]{:S(2)}, u32[]{:S(2)}) %collective-permute-start) | collective-permute-done | bytes 4194336 | tf_op jit(solution)/shard_map/ppermute | solution.py:208
  255.0 13.3 %copy.175 = f32[2,16,2,128,256]{4,2,1,0,3:T(2,128)} copy(f32[2,16,2,128,256]{3,4,0,1,2:T(8,128)} %pad_maximum_fusion.1) | data formatting | bytes 16777216 | tf_op jit(solution)/shard_map/stack | solution.py:213
  268.3 10.9 %reshape.2175 = f32[2,32,128,256,1,1]{3,1,0,2,4,5:T(8,128)} reshape(f32[2,16,2,128,256]{4,2,1,0,3:T(2,128)} %copy.175) | data formatting | bytes 16777216 | tf_op jit(solution)/shard_map/reshape;reshape | solution.py:94
  279.2 16.7 %fusion.19 = f32[2,32,2,128,256]{4,1,3,2,0:T(8,128)S(1)} fusion(f32[2,32,128,256,1,1]{3,1,0,2,4,5:T(8,128)} %reshape.2175, f32[1,2,2,32,32]{4,3,2,1,0:T(8,128)S(1)} %fusion.98, f32[1,2,2,32,32]{4,3,2,1,0:T(8,128)S(1)} %maximum_bitcast_fusion.31), kind=kOutput, calls=%fused_computation.30 | convolution fusion | flops 3221233664 | bytes 25198592 | tf_op jit(solution)/shard_map/oafeb,ebnj->oafnj/dot_general | solution.py:96
  295.9 6.0 subtract_bitcast_fusion
  306.9 25.0 %fusion.22 = f32[2,2,128,32,256]{4,2,3,1,0:T(8,128)S(1)} fusion(f32[2,32,2,128,256,1]{4,1,3,0,2,5:T(8,128)S(1)} %maximum_bitcast_fusion, f32[1,2,2,128,128]{4,3,2,1,0:T(8,128)} %maximum_bitcast_fusion.12, f32[1,2,2,128,128]{4,3,2,1,0:T(8,128)} %maximum_bitcast_fusion.11), kind=kOutput, calls=%fused_computation.31 | convolution fusion | flops 12885032960 | bytes 34078720 | tf_op jit(solution)/shard_map/ofekn,oaenj->ofkaj/dot_general | solution.py:106
  331.9 5.8 copy-done.3
  342.1 8.2 %copy.181 = f32[1,2,128,32,256]{4,3,2,1,0:T(8,128)S(1)} copy(f32[1,2,128,32,256]{4,2,3,1,0:T(8,128)} %slice.369) | data formatting | bytes 16777216 | tf_op jit(solution)/shard_map/slice | solution.py:228
  367.5 11.5 %copy.166 = bf16[1,2,2,16,256,256]{5,4,3,2,1,0:T(8,128)(2,1)} copy(bf16[1,2,2,16,256,256]{4,5,2,1,3,0:T(8,128)(2,1)} %bitcast.54) | data formatting | bytes 16777216 | tf_op jit(solution)/shard_map/all_to_all | solution.py:222
  379.0 11.1 %fusion.32 = (f32[1,4096,256]{2,1,0:T(8,128)S(1)}, f32[1,4096,256]{2,1,0:T(8,128)S(1)}) fusion(bf16[2,2,4096,256]{3,2,1,0:T(8,128)(2,1)} %bitcast.577, f32[]{:T(128)} %bitcast.125, f32[]{:T(128)} %bitcast.124, f32[2,4096,256]{2,1,0:T(8,128)} %maximum_select_fusion, f32[1,1,128,32,256]{4,3,2,1,0:T(8,128)} %copy.180, f32[]{:T(128)} %bitcast.130, f32[]{:T(128)} %bitcast.129, ...), kind=kLoop, calls=%fused_computation.49 | loop fusion | flops 36700160 | bytes 33554448 | tf_op jit(solution)/shard_map/sub | solution.py:244
  395.0 7.7 %fusion.47 = f32[32,2,128,256]{3,0,2,1:T(8,128)S(1)} fusion(f32[1,32,128,256]{3,1,0,2:T(8,128)S(1)} %copy.184, f32[1,32,128,256]{3,1,0,2:T(8,128)S(1)} %copy.183, f32[1,2,32,32]{3,2,1,0:T(8,128)S(1)} %copy-done.17, f32[1,2,32,32]{3,2,1,0:T(8,128)S(1)} %copy-done.15), kind=kOutput, calls=%fused_computation.90 | convolution fusion | flops 1612713984 | bytes 16793600 | tf_op jit(solution)/shard_map/afeb,ebnj->afnj/dot_general | solution.py:115
  405.9 9.4 %fusion.57 = f32[2,16,32,256]{3,1,2,0:T(8,128)S(1)} fusion(f32[32,2,128,256]{3,0,2,1:T(8,128)S(1)} %pad_maximum_fusion.2, f32[1,2,16,128]{3,2,1,0:T(8,128)S(1)} %copy-done.25, f32[1,2,16,128]{3,2,1,0:T(8,128)S(1)} %copy-done.24), kind=kOutput, calls=%fused_computation.111 | convolution fusion | flops 805314560 | bytes 9469952 | tf_op jit(solution)/shard_map/fken,aenj->fkaj/dot_general | solution.py:125
  416.8 10.7 %fusion.60 = f32[2,16,32,256]{3,1,2,0:T(8,128)} fusion(f32[32,2,128,256]{3,0,2,1:T(8,128)S(1)} %pad_maximum_fusion.2, f32[1,2,16,128]{3,2,1,0:T(8,128)S(1)} %copy-done.27, f32[1,2,16,128]{3,2,1,0:T(8,128)S(1)} %copy-done.26), kind=kOutput, calls=%fused_computation.112 | convolution fusion | flops 805314560 | bytes 9469952 | tf_op jit(solution)/shard_map/fken,aenj->fkaj/dot_general | solution.py:125
  428.1 10.5 %fusion.63 = f32[2,16,32,256]{3,1,2,0:T(8,128)} fusion(f32[32,2,128,256]{3,0,2,1:T(8,128)S(1)} %pad_maximum_fusion.2, f32[1,2,16,128]{3,2,1,0:T(8,128)S(1)} %copy-done.29, f32[1,2,16,128]{3,2,1,0:T(8,128)S(1)} %copy-done.28), kind=kOutput, calls=%fused_computation.113 | convolution fusion | flops 805314560 | bytes 9469952 | tf_op jit(solution)/shard_map/fken,aenj->fkaj/dot_general | solution.py:125
  440.1 10.5 %fusion.66 = f32[2,16,32,256]{3,1,2,0:T(8,128)} fusion(f32[32,2,128,256]{3,0,2,1:T(8,128)S(1)} %pad_maximum_fusion.2, f32[1,2,16,128]{3,2,1,0:T(8,128)S(1)} %copy-done.31, f32[1,2,16,128]{3,2,1,0:T(8,128)S(1)} %copy-done.30), kind=kOutput, calls=%fused_computation.114 | convolution fusion | flops 805314560 | bytes 9469952 | tf_op jit(solution)/shard_map/fken,aenj->fkaj/dot_general | solution.py:125
  451.6 13.0 %fusion.48 = f32[2,64,32,256]{3,1,2,0:T(8,128)S(1)} fusion(f32[32,2,128,256]{3,0,2,1:T(8,128)} %copy-done.2, f32[1,2,64,128]{3,2,1,0:T(8,128)S(1)} %get-tuple-element.164, f32[1,2,64,128]{3,2,1,0:T(8,128)S(1)} %get-tuple-element.163), kind=kOutput, calls=%fused_computation.92 | convolution fusion | flops 3221258240 | bytes 12713984 | tf_op jit(solution)/shard_map/fken,aenj->fkaj/dot_general | solution.py:125
  467.1 19.4 %collective-permute-done.3 = f32[2,16,32,256]{3,1,2,0:T(8,128)} collective-permute-done((f32[2,16,32,256]{3,1,2,0:T(8,128)}, f32[2,16,32,256]{3,1,2,0:T(8,128)}, u32[]{:S(2)}, u32[]{:S(2)}) %collective-permute-start.3) | collective-permute-done | bytes 1048608 | tf_op jit(solution)/shard_map/ppermute | solution.py:260
  486.5 20.7 %collective-permute-done.4 = f32[2,16,32,256]{3,1,2,0:T(8,128)} collective-permute-done((f32[2,16,32,256]{3,1,2,0:T(8,128)}, f32[2,16,32,256]{3,1,2,0:T(8,128)}, u32[]{:S(2)}, u32[]{:S(2)}) %collective-permute-start.4) | collective-permute-done | bytes 1048608 | tf_op jit(solution)/shard_map/ppermute | solution.py:260
  507.2 6.0 maximum_add_fusion
  517.7 6.0 all-to-all-start.2
  524.6 91.5 %all-to-all-done.2 = f32[2,16,128,256]{3,2,0,1:T(8,128)} async-done(((f32[2,16,128,256]{3,2,0,1:T(8,128)}), f32[2,16,128,256]{3,2,0,1:T(8,128)}, u32[]{:S(2)}, u32[]{:S(2)}) %all-to-all-start.2) | async-done | bytes 4194336 | tf_op jit(solution)/shard_map/all_to_all | solution.py:269
  616.0 18.1 %convolution_bitcast_fusion = f32[2,32,2,128,256]{4,1,3,2,0:T(8,128)S(1)} fusion(f32[2,16,128,256,1,1]{3,2,0,1,5,4:T(8,128)} %bitcast.181, f32[1,2,2,32,16]{3,4,2,1,0:T(8,128)S(1)} %maximum_bitcast_fusion.45, f32[1,2,2,32,16]{3,4,2,1,0:T(8,128)S(1)} %maximum_bitcast_fusion.44), kind=kOutput, calls=%fused_computation.32 | convolution fusion | flops 1610616832 | bytes 20987904 | tf_op jit(solution)/shard_map/oafem,emRj->oafRj/dot_general | solution.py:147
  639.9 6.9 fusion.38
  646.8 7.1 fusion.51
  657.2 8.1 %fusion.40 = f32[32,128,2,64,1]{1,3,4,2,0:T(8,128)S(1)} fusion(f32[32,2,128,128,1]{3,0,2,1,4:T(8,128)} %copy-done.6, f32[2,2,128,2,64]{2,4,1,3,0:T(8,128)S(1)} %fusion.75), kind=kOutput, calls=%fused_computation.83 | convolution fusion | flops 1610612736 | bytes 6422528 | tf_op jit(solution)/shard_map/aeRu,eufk->aRfk/dot_general | solution.py:165
  665.3 6.9 fusion.52
  673.4 29.8 %collective-permute-done.5 = f32[2,128,2048]{1,2,0:T(8,128)} collective-permute-done((f32[2,128,2048]{1,2,0:T(8,128)S(1)}, f32[2,128,2048]{1,2,0:T(8,128)}, u32[]{:S(2)}, u32[]{:S(2)}) %collective-permute-start.5) | collective-permute-done | bytes 2097184 | tf_op jit(solution)/shard_map/ppermute | solution.py:273
  (248 shorter events, 170.6 us)
Async XLA Ops:
  0.0 150.5 %copy-start = (f32[4,2]{0,1:T(2,128)S(1)}, f32[4,2]{0,1:T(2,128)}, u32[]{:S(2)}) copy-start(f32[4,2]{0,1:T(2,128)} %param.23) | copy-start | bytes 100
  29.0 3.5 copy-start.35
  39.4 98.6 %all-to-all-start.1 = ((f32[16,2,128,256]{2,3,1,0:T(8,128)}), f32[16,2,128,256]{2,3,1,0:T(8,128)}, u32[]{:S(2)}, u32[]{:S(2)}) async-start(f32[16,2,128,256]{2,3,1,0:T(8,128)} %scatter.4), calls=%async_computation.1 | async-start | bytes 8388608 | tf_op jit(solution)/shard_map/all_to_all | solution.py:207
  45.7 47.5 %copy-start.32 = (pred[128]{0:T(512)(128)(4,1)}, pred[128]{0:T(512)(128)(4,1)S(1)}, u32[]{:S(2)}) copy-start(pred[128]{0:T(512)(128)(4,1)S(1)} %get-tuple-element.218) | copy-start | bytes 388
  57.3 8.8 %copy-start.8 = (bf16[2,2,256,128]{3,2,1,0:T(8,128)(2,1)S(1)}, bf16[2,2,256,128]{3,2,1,0:T(8,128)(2,1)}, u32[]{:S(2)}) copy-start(bf16[2,2,256,128]{3,2,1,0:T(8,128)(2,1)} %get-tuple-element.143) | copy-start | bytes 786436
  84.5 8.7 %copy-start.34 = (s32[128]{0:T(128)S(1)}, s32[128]{0:T(128)}, u32[]{:S(2)}) copy-start(s32[128]{0:T(128)} %iota_subtract_fusion) | copy-start | bytes 1540
  138.0 229.5 %all-to-all-start = ((bf16[16,2,2,256,256]{3,4,2,1,0:T(8,128)(2,1)}), bf16[16,2,2,256,256]{3,4,2,1,0:T(8,128)(2,1)}, u32[]{:S(2)}, u32[]{:S(2)}) async-start(bf16[16,2,2,256,256]{3,4,2,1,0:T(8,128)(2,1)} %pad_maximum_fusion), calls=%async_computation | async-start | bytes 16777216 | tf_op jit(solution)/shard_map/all_to_all | solution.py:222
  143.4 6.9 copy-start.13
  143.4 7.0 copy-start.11
  148.7 92.9 %collective-permute-start = (f32[2,2048,256]{2,1,0:T(8,128)}, f32[2,2048,256]{2,1,0:T(8,128)}, u32[]{:S(2)}, u32[]{:S(2)}) collective-permute-start(f32[2,2048,256]{2,1,0:T(8,128)} %bitcast.586), channel_id=1, source_target_pairs={{0,16},{16,0},{1,17},{17,1},{2,18},{18,2},{3,19},{19,3},{4,20},{20... | collective-permute-start | bytes 12582920 | tf_op jit(solution)/shard_map/ppermute | solution.py:208
  153.8 5.6 copy-start.20
  153.8 5.6 copy-start.22
  331.9 5.8 copy-start.3
  395.0 7.7 %copy-start.18 = (f32[32,128]{0,1:T(8,128)S(1)}, f32[32,128]{0,1:T(8,128)}, u32[]{:S(2)}) copy-start(f32[32,128]{0,1:T(8,128)} %copy.185) | copy-start | bytes 49156
  395.0 7.7 %copy-start.19 = (f32[32,128]{0,1:T(8,128)S(1)}, f32[32,128]{0,1:T(8,128)}, u32[]{:S(2)}) copy-start(f32[32,128]{0,1:T(8,128)} %copy.186) | copy-start | bytes 49156
  405.8 34.3 %copy-start.2 = (f32[32,2,128,256]{3,0,2,1:T(8,128)}, f32[32,2,128,256]{3,0,2,1:T(8,128)S(1)}, u32[]{:S(2)}) copy-start(f32[32,2,128,256]{3,0,2,1:T(8,128)S(1)} %pad_maximum_fusion.2) | copy-start | bytes 25165828
  405.9 11.0 %copy-start.26 = (f32[1,2,16,128]{3,2,1,0:T(8,128)S(1)}, f32[1,2,16,128]{3,2,1,0:T(8,128)}, u32[]{:S(2)}) copy-start(f32[1,2,16,128]{3,2,1,0:T(8,128)} %get-tuple-element.179) | copy-start | bytes 49156
  405.9 11.0 %copy-start.27 = (f32[1,2,16,128]{3,2,1,0:T(8,128)S(1)}, f32[1,2,16,128]{3,2,1,0:T(8,128)}, u32[]{:S(2)}) copy-start(f32[1,2,16,128]{3,2,1,0:T(8,128)} %get-tuple-element.180) | copy-start | bytes 49156
  415.2 51.8 %collective-permute-start.1 = (f32[2,16,32,256]{3,1,2,0:T(8,128)S(1)}, f32[2,16,32,256]{3,1,2,0:T(8,128)S(1)}, u32[]{:S(2)}, u32[]{:S(2)}) collective-permute-start(f32[2,16,32,256]{3,1,2,0:T(8,128)S(1)} %fusion.57), channel_id=1, source_target_pairs={{0,16},{16,0},{1,17},{17,1},{2,18},{18,2},{3,19},{19,3},{4,20},{20... | collective-permute-start | bytes 3145736 | tf_op jit(solution)/shard_map/ppermute | solution.py:260
  416.8 11.3 %copy-start.28 = (f32[1,2,16,128]{3,2,1,0:T(8,128)S(1)}, f32[1,2,16,128]{3,2,1,0:T(8,128)}, u32[]{:S(2)}) copy-start(f32[1,2,16,128]{3,2,1,0:T(8,128)} %get-tuple-element.181) | copy-start | bytes 49156
  416.8 11.3 %copy-start.29 = (f32[1,2,16,128]{3,2,1,0:T(8,128)S(1)}, f32[1,2,16,128]{3,2,1,0:T(8,128)}, u32[]{:S(2)}) copy-start(f32[1,2,16,128]{3,2,1,0:T(8,128)} %get-tuple-element.182) | copy-start | bytes 49156
  427.6 39.5 %collective-permute-start.2 = (f32[2,16,32,256]{3,1,2,0:T(8,128)}, f32[2,16,32,256]{3,1,2,0:T(8,128)S(1)}, u32[]{:S(2)}, u32[]{:S(2)}) collective-permute-start(f32[2,16,32,256]{3,1,2,0:T(8,128)} %fusion.60), channel_id=1, source_target_pairs={{0,16},{16,0},{1,17},{17,1},{2,18},{18,2},{3,19},{19,3},{4,20},{20... | collective-permute-start | bytes 3145736 | tf_op jit(solution)/shard_map/ppermute | solution.py:260
  428.1 12.0 %copy-start.30 = (f32[1,2,16,128]{3,2,1,0:T(8,128)S(1)}, f32[1,2,16,128]{3,2,1,0:T(8,128)}, u32[]{:S(2)}) copy-start(f32[1,2,16,128]{3,2,1,0:T(8,128)} %get-tuple-element.183) | copy-start | bytes 49156
  428.1 12.0 %copy-start.31 = (f32[1,2,16,128]{3,2,1,0:T(8,128)S(1)}, f32[1,2,16,128]{3,2,1,0:T(8,128)}, u32[]{:S(2)}) copy-start(f32[1,2,16,128]{3,2,1,0:T(8,128)} %get-tuple-element.184) | copy-start | bytes 49156
  438.6 47.9 %collective-permute-start.3 = (f32[2,16,32,256]{3,1,2,0:T(8,128)}, f32[2,16,32,256]{3,1,2,0:T(8,128)}, u32[]{:S(2)}, u32[]{:S(2)}) collective-permute-start(f32[2,16,32,256]{3,1,2,0:T(8,128)} %fusion.63), channel_id=1, source_target_pairs={{0,16},{16,0},{1,17},{17,1},{2,18},{18,2},{3,19},{19,3},{4,20},{20... | collective-permute-start | bytes 3145736 | tf_op jit(solution)/shard_map/ppermute | solution.py:260
  450.6 56.6 %collective-permute-start.4 = (f32[2,16,32,256]{3,1,2,0:T(8,128)}, f32[2,16,32,256]{3,1,2,0:T(8,128)}, u32[]{:S(2)}, u32[]{:S(2)}) collective-permute-start(f32[2,16,32,256]{3,1,2,0:T(8,128)} %fusion.66), channel_id=1, source_target_pairs={{0,16},{16,0},{1,17},{17,1},{2,18},{18,2},{3,19},{19,3},{4,20},{20... | collective-permute-start | bytes 3145736 | tf_op jit(solution)/shard_map/ppermute | solution.py:260
  517.7 98.3 %all-to-all-start.2 = ((f32[2,16,128,256]{3,2,0,1:T(8,128)}), f32[2,16,128,256]{3,2,0,1:T(8,128)}, u32[]{:S(2)}, u32[]{:S(2)}) async-start(f32[2,16,128,256]{3,2,0,1:T(8,128)} %copy.194), calls=%async_computation.2 | async-start | bytes 8388608 | tf_op jit(solution)/shard_map/all_to_all | solution.py:269
  638.8 8.1 %copy-start.4 = (f32[32,2,128,128,1]{3,0,2,1,4:T(8,128)}, f32[32,2,128,128,1]{3,0,2,1,4:T(8,128)S(1)}, u32[]{:S(2)}) copy-start(f32[32,2,128,128,1]{3,0,2,1,4:T(8,128)S(1)} %maximum_bitcast_fusion.4) | copy-start | bytes 12582916
  639.9 14.0 %copy-start.6 = (f32[32,2,128,128,1]{3,0,2,1,4:T(8,128)}, f32[32,2,128,128,1]{3,0,2,1,4:T(8,128)S(1)}, u32[]{:S(2)}) copy-start(f32[32,2,128,128,1]{3,0,2,1,4:T(8,128)S(1)} %maximum_bitcast_fusion.5) | copy-start | bytes 12582916
  655.2 48.0 %collective-permute-start.5 = (f32[2,128,2048]{1,2,0:T(8,128)S(1)}, f32[2,128,2048]{1,2,0:T(8,128)}, u32[]{:S(2)}, u32[]{:S(2)}) collective-permute-start(f32[2,128,2048]{1,2,0:T(8,128)S(1)} %bitcast.587), channel_id=1, source_target_pairs={{0,16},{16,0},{1,17},{17,1},{2,18},{18,2},{3,19},{19,3},{4,20},{20... | collective-permute-start | bytes 6291464 | tf_op jit(solution)/shard_map/ppermute | solution.py:273
  656.8 8.5 %copy-start.5 = (f32[32,2,128,128,1]{3,0,2,1,4:T(8,128)S(1)}, f32[32,2,128,128,1]{3,0,2,1,4:T(8,128)}, u32[]{:S(2)}) copy-start(f32[32,2,128,128,1]{3,0,2,1,4:T(8,128)} %copy-done.4) | copy-start | bytes 12582916
  705.1 7.7 %copy-start.1 = (f32[4,2]{0,1:T(2,128)S(1)}, f32[4,2]{0,1:T(2,128)}, u32[]{:S(2)}) copy-start(f32[4,2]{0,1:T(2,128)} %param.23) | copy-start | bytes 100
  (13 other events, 21.9 us)
where the time goes:
time: 724 us; the launch traced here: 713 us
  waiting for transfers between devices  274 us (38%)
  matrix products  178 us (25%)
  local copies, waits for them, and re-layouts  159 us (22%)
  other arithmetic  72.8 us (10%)
  starting transfers between devices  24.9 us (3%)
    all_to_all x1, waiting for transfers between devices, local(): lax.all_to_all(summed, 'row', split_axis=1, concat_axis=1, tiled=True)  91.5 us
    ppermute x1, waiting for transfers between devices, local(): other = lax.ppermute(got, 'wl', perm=[(0, 1), (1, 0)])  80.8 us
    dot_general x5, matrix products, inverse_cols_half(): jnp.einsum('fken,aenj->fkaj', second_tab, turned, precision=PRECISE)  54.1 us
    unnamed x118, local copies, waits for them, and re-layouts  48.7 us
    ppermute x4, waiting for transfers between devices, local(): incoming.append(lax.ppermute(given, 'wl', perm=[(0, 1), (1, 0)]))  40.1 us
    all_to_all x1, waiting for transfers between devices, local(): lax.all_to_all(sent, 'row', split_axis=0, concat_axis=2, tiled=True)[0]  32.1 us
    ppermute x1, waiting for transfers between devices, local(): taken = lax.ppermute(theirs, 'wl', perm=[(0, 1), (1, 0)])  29.8 us
    dot_general x1, matrix products, forward_cols(): jnp.einsum('ofekn,oaenj->ofkaj', second_tab, turned, precision=PRECISE)  25 us
  transfers between devices with their start and end apart: 9, of which 6 were waited for; matrix products, arithmetic and copies ran while one was open for 36% of the time, Pallas kernels for 0%

commit v1 on v0

--- a/solution.py
+++ b/solution.py
@@ -266,7 +266,26 @@
         given = lax.dynamic_index_in_dim(back, 1 - wl_index, 2, keepdims=False)
         incoming = lax.ppermute(given, "wl", perm=[(0, 1), (1, 0)])
     summed = kept + incoming
-    returned = lax.all_to_all(summed, "row", split_axis=1, concat_axis=1, tiled=True)
+
+    def _balance_tasks(t0):
+        mesh_name = "row"
+        work_now, later = (lax.axis_size(mesh_name), lax.axis_index(mesh_name))
+        carry_out = t0.shape[1] // work_now
+        aux = list(t0.shape)
+        aux[1] = carry_out
+        z2 = aux[1]
+        aux[1] = z2 * work_now
+        w1 = jnp.zeros(aux, t0.dtype)
+        for i0 in range(work_now):
+            finding = lax.dynamic_slice_in_dim(t0, (later ^ i0) * carry_out, carry_out, axis=1)
+            if i0:
+                finding = lax.ppermute(
+                    finding, mesh_name, [(nth, nth ^ i0) for nth in range(work_now)]
+                )
+            w1 = lax.dynamic_update_slice_in_dim(w1, finding, (later ^ i0) * z2, axis=1)
+        return w1
+
+    returned = _balance_tasks(summed)
     returned = groups_to_canon(returned, mcount, 1)
     k_half = across // 2
     theirs = inverse_rows(returned, length, norm_factor, k_half, (1 - wl_index) * k_half)

time: 724 us -> 739 us (1.021)
  local copies, waits for them, and re-layouts: 159 us -> 192 us
  waiting for transfers between devices: 274 us -> 245 us
  starting transfers between devices: 24.9 us -> 34.4 us
    all_to_all x1 -> x0, waiting for transfers between devices: 91.5 us -> none  [local(): lax.all_to_all(summed, 'row', split_axis=1, concat_axis=1, tiled=True)]
    ppermute x0 -> x15, waiting for transfers between devices: none -> 65.1 us  [_balance_tasks(): lax.ppermute(finding, mesh_name, [(nth, nth ^ i0) for nth in range(work_n...]
    dynamic_update_slice x0 -> x17, local copies, waits for them, and re-layouts: none -> 17.1 us  [_balance_tasks(): w1 = lax.dynamic_update_slice_in_dim(w1, finding, (later ^ i0) * z2, axis=1)]
    ppermute x0 -> x15, starting transfers between devices: none -> 15.9 us  [_balance_tasks(): lax.ppermute(finding, mesh_name, [(nth, nth ^ i0) for nth in range(work_n...]
    ppermute x0 -> x15, local copies, waits for them, and re-layouts: none -> 11.7 us  [_balance_tasks(): lax.ppermute(finding, mesh_name, [(nth, nth ^ i0) for nth in range(work_n...]
    unnamed x118 -> x136, local copies, waits for them, and re-layouts: 48.7 us -> 49 us
  transfers between devices with their start and end apart: 9 -> 23, of which waited for: 6 -> 14; matrix products, arithmetic and copies ran while one was open for 36% -> 40% of each run, Pallas kernels for 0% -> 0%
where the time goes in v1:
time: 739 us; the launch traced here: 726 us
  waiting for transfers between devices  245 us (33%)
  local copies, waits for them, and re-layouts  192 us (26%)
  matrix products  176 us (24%)
  other arithmetic  74.4 us (10%)
  starting transfers between devices  34.4 us (5%)
    ppermute x1, waiting for transfers between devices, local(): other = lax.ppermute(got, 'wl', perm=[(0, 1), (1, 0)])  78 us
    ppermute x15, waiting for transfers between devices, _balance_tasks(): lax.ppermute(finding, mesh_name, [(nth, nth ^ i0) for nth in range(work_n...  65.1 us
    dot_general x5, matrix products, inverse_cols_half(): jnp.einsum('fken,aenj->fkaj', second_tab, turned, precision=PRECISE)  54.1 us
    unnamed x136, local copies, waits for them, and re-layouts  49 us
    ppermute x4, waiting for transfers between devices, local(): incoming.append(lax.ppermute(given, 'wl', perm=[(0, 1), (1, 0)]))  39.9 us
    all_to_all x1, waiting for transfers between devices, local(): lax.all_to_all(sent, 'row', split_axis=0, concat_axis=2, tiled=True)[0]  32.1 us
    ppermute x1, waiting for transfers between devices, local(): taken = lax.ppermute(theirs, 'wl', perm=[(0, 1), (1, 0)])  29.4 us
    dot_general x1, matrix products, forward_cols(): jnp.einsum('ofekn,oaenj->ofkaj', second_tab, turned, precision=PRECISE)  25.4 us
  transfers between devices with their start and end apart: 23, of which 14 were waited for; matrix products, arithmetic and copies ran while one was open for 40% of the time, Pallas kernels for 0%

profile of v1, /device:TPU:10, one launch (start us, length us, event | category | flops | bytes accessed | tf_op | source)
XLA Modules:
  0.0 726.0 jit_solution(9026867601987635477)
XLA Ops:
  5.0 6.8 fusion.45
  14.9 13.9 %fusion.17 = f32[2,32,128,2,64,1]{2,4,5,3,1,0:T(8,128)S(1)} fusion(f32[2,32,2,128,128,1]{4,1,3,0,2,5:T(8,128)S(1)} %maximum_bitcast_fusion.1, f32[1,2,2,64,128]{4,3,2,1,0:T(8,128)S(1)} %maximum_bitcast_fusion.22, f32[1,2,2,64,128]{4,3,2,1,0:T(8,128)S(1)} %maximum_bitcast_fusion.21), kind=kOutput, calls=%fused_computation.26 | convolution fusion | flops 3221291008 | bytes 12845056 | tf_op jit(solution)/shard_map/oaern,oenfk->oarfk/dot_general | solution.py:80
  39.2 6.2 all-to-all-start.1
  97.9 7.8 %pad_maximum_fusion = bf16[16,2,2,256,256]{3,4,2,1,0:T(8,128)(2,1)} fusion(bf16[16,2,2,256,128]{3,4,2,1,0:T(8,128)(2,1)} %convolution_convert_fusion, bf16[16,2,2,256,128]{3,4,2,1,0:T(8,128)(2,1)} %bitcast_dynamic-update-slice_fusion.15), kind=kLoop, calls=%fused_computation.5 | loop fusion | flops 16777216 | bytes 16777216 | tf_op jit(solution)/shard_map/concatenate | solution.py:187
  105.7 32.1 %all-to-all-done.1 = f32[16,2,128,256]{2,3,1,0:T(8,128)} async-done(((f32[16,2,128,256]{2,3,1,0:T(8,128)}), f32[16,2,128,256]{2,3,1,0:T(8,128)}, u32[]{:S(2)}, u32[]{:S(2)}) %all-to-all-start.1) | async-done | bytes 4194336 | tf_op jit(solution)/shard_map/all_to_all | solution.py:207
  163.4 78.0 %collective-permute-done = f32[2,2048,256]{2,1,0:T(8,128)} collective-permute-done((f32[2,2048,256]{2,1,0:T(8,128)}, f32[2,2048,256]{2,1,0:T(8,128)}, u32[]{:S(2)}, u32[]{:S(2)}) %collective-permute-start) | collective-permute-done | bytes 4194336 | tf_op jit(solution)/shard_map/ppermute | solution.py:208
  254.7 13.3 %copy.152 = f32[2,16,2,128,256]{4,2,1,0,3:T(2,128)} copy(f32[2,16,2,128,256]{3,4,0,1,2:T(8,128)} %pad_maximum_fusion.1) | data formatting | bytes 16777216 | tf_op jit(solution)/shard_map/stack | solution.py:213
  268.0 10.9 %reshape.2175 = f32[2,32,128,256,1,1]{3,1,0,2,4,5:T(8,128)} reshape(f32[2,16,2,128,256]{4,2,1,0,3:T(2,128)} %copy.152) | data formatting | bytes 16777216 | tf_op jit(solution)/shard_map/reshape;reshape | solution.py:94
  278.9 17.1 %fusion.19 = f32[2,32,2,128,256]{4,1,3,2,0:T(8,128)S(1)} fusion(f32[2,32,128,256,1,1]{3,1,0,2,4,5:T(8,128)} %reshape.2175, f32[1,2,2,32,32]{4,3,2,1,0:T(8,128)S(1)} %fusion.97, f32[1,2,2,32,32]{4,3,2,1,0:T(8,128)S(1)} %maximum_bitcast_fusion.31), kind=kOutput, calls=%fused_computation.30 | convolution fusion | flops 3221233664 | bytes 25198592 | tf_op jit(solution)/shard_map/oafeb,ebnj->oafnj/dot_general | solution.py:96
  306.6 25.4 %fusion.22 = f32[2,2,128,32,256]{4,2,3,1,0:T(8,128)S(1)} fusion(f32[2,32,2,128,256,1]{4,1,3,0,2,5:T(8,128)S(1)} %maximum_bitcast_fusion, f32[1,2,2,128,128]{4,3,2,1,0:T(8,128)} %maximum_bitcast_fusion.12, f32[1,2,2,128,128]{4,3,2,1,0:T(8,128)} %maximum_bitcast_fusion.11), kind=kOutput, calls=%fused_computation.31 | convolution fusion | flops 12885032960 | bytes 34078720 | tf_op jit(solution)/shard_map/ofekn,oaenj->ofkaj/dot_general | solution.py:106
  332.0 5.8 copy-done.3
  342.2 8.2 %copy.158 = f32[1,2,128,32,256]{4,3,2,1,0:T(8,128)S(1)} copy(f32[1,2,128,32,256]{4,2,3,1,0:T(8,128)} %slice.369) | data formatting | bytes 16777216 | tf_op jit(solution)/shard_map/slice | solution.py:228
  367.6 11.4 %copy.143 = bf16[1,2,2,16,256,256]{5,4,3,2,1,0:T(8,128)(2,1)} copy(bf16[1,2,2,16,256,256]{4,5,2,1,3,0:T(8,128)(2,1)} %bitcast.54) | data formatting | bytes 16777216 | tf_op jit(solution)/shard_map/all_to_all | solution.py:222
  379.0 10.8 %fusion.32 = (f32[1,4096,256]{2,1,0:T(8,128)S(1)}, f32[1,4096,256]{2,1,0:T(8,128)S(1)}) fusion(bf16[2,2,4096,256]{3,2,1,0:T(8,128)(2,1)} %bitcast.580, f32[]{:T(128)} %bitcast.125, f32[]{:T(128)} %bitcast.124, f32[2,4096,256]{2,1,0:T(8,128)} %maximum_select_fusion, f32[1,1,128,32,256]{4,3,2,1,0:T(8,128)} %copy.157, f32[]{:T(128)} %bitcast.130, f32[]{:T(128)} %bitcast.129, ...), kind=kLoop, calls=%fused_computation.49 | loop fusion | flops 36700160 | bytes 33554448 | tf_op jit(solution)/shard_map/sub | solution.py:244
  394.8 7.9 %fusion.46 = f32[32,2,128,256]{3,0,2,1:T(8,128)S(1)} fusion(f32[1,32,128,256]{3,1,0,2:T(8,128)S(1)} %copy.161, f32[1,32,128,256]{3,1,0,2:T(8,128)S(1)} %copy.160, f32[1,2,32,32]{3,2,1,0:T(8,128)S(1)} %copy-done.17, f32[1,2,32,32]{3,2,1,0:T(8,128)S(1)} %copy-done.15), kind=kOutput, calls=%fused_computation.89 | convolution fusion | flops 1612713984 | bytes 16793600 | tf_op jit(solution)/shard_map/afeb,ebnj->afnj/dot_general | solution.py:115
  405.9 9.4 %fusion.56 = f32[2,16,32,256]{3,1,2,0:T(8,128)S(1)} fusion(f32[32,2,128,256]{3,0,2,1:T(8,128)S(1)} %pad_maximum_fusion.2, f32[1,2,16,128]{3,2,1,0:T(8,128)S(1)} %copy-done.32, f32[1,2,16,128]{3,2,1,0:T(8,128)S(1)} %copy-done.31), kind=kOutput, calls=%fused_computation.110 | convolution fusion | flops 805314560 | bytes 9469952 | tf_op jit(solution)/shard_map/fken,aenj->fkaj/dot_general | solution.py:125
  416.9 10.5 %fusion.59 = f32[2,16,32,256]{3,1,2,0:T(8,128)} fusion(f32[32,2,128,256]{3,0,2,1:T(8,128)S(1)} %pad_maximum_fusion.2, f32[1,2,16,128]{3,2,1,0:T(8,128)S(1)} %copy-done.30, f32[1,2,16,128]{3,2,1,0:T(8,128)S(1)} %copy-done.29), kind=kOutput, calls=%fused_computation.111 | convolution fusion | flops 805314560 | bytes 9469952 | tf_op jit(solution)/shard_map/fken,aenj->fkaj/dot_general | solution.py:125
  427.9 10.5 %fusion.62 = f32[2,16,32,256]{3,1,2,0:T(8,128)} fusion(f32[32,2,128,256]{3,0,2,1:T(8,128)S(1)} %pad_maximum_fusion.2, f32[1,2,16,128]{3,2,1,0:T(8,128)S(1)} %copy-done.36, f32[1,2,16,128]{3,2,1,0:T(8,128)S(1)} %copy-done.35), kind=kOutput, calls=%fused_computation.112 | convolution fusion | flops 805314560 | bytes 9469952 | tf_op jit(solution)/shard_map/fken,aenj->fkaj/dot_general | solution.py:125
  439.9 10.8 %fusion.65 = f32[2,16,32,256]{3,1,2,0:T(8,128)} fusion(f32[32,2,128,256]{3,0,2,1:T(8,128)S(1)} %pad_maximum_fusion.2, f32[1,2,16,128]{3,2,1,0:T(8,128)S(1)} %copy-done.34, f32[1,2,16,128]{3,2,1,0:T(8,128)S(1)} %copy-done.33), kind=kOutput, calls=%fused_computation.113 | convolution fusion | flops 805314560 | bytes 9469952 | tf_op jit(solution)/shard_map/fken,aenj->fkaj/dot_general | solution.py:125
  451.8 13.0 %fusion.47 = f32[2,64,32,256]{3,1,2,0:T(8,128)S(1)} fusion(f32[32,2,128,256]{3,0,2,1:T(8,128)} %copy-done.2, f32[1,2,64,128]{3,2,1,0:T(8,128)S(1)} %get-tuple-element.180, f32[1,2,64,128]{3,2,1,0:T(8,128)S(1)} %get-tuple-element.179), kind=kOutput, calls=%fused_computation.91 | convolution fusion | flops 3221258240 | bytes 12713984 | tf_op jit(solution)/shard_map/fken,aenj->fkaj/dot_general | solution.py:125
  467.3 19.2 %collective-permute-done.3 = f32[2,16,32,256]{3,1,2,0:T(8,128)} collective-permute-done((f32[2,16,32,256]{3,1,2,0:T(8,128)}, f32[2,16,32,256]{3,1,2,0:T(8,128)}, u32[]{:S(2)}, u32[]{:S(2)}) %collective-permute-start.3) | collective-permute-done | bytes 1048608 | tf_op jit(solution)/shard_map/ppermute | solution.py:260
  486.5 20.8 %collective-permute-done.4 = f32[2,16,32,256]{3,1,2,0:T(8,128)} collective-permute-done((f32[2,16,32,256]{3,1,2,0:T(8,128)}, f32[2,16,32,256]{3,1,2,0:T(8,128)}, u32[]{:S(2)}, u32[]{:S(2)}) %collective-permute-start.4) | collective-permute-done | bytes 1048608 | tf_op jit(solution)/shard_map/ppermute | solution.py:260
  542.8 7.4 %collective-permute-done.10 = f32[2,1,128,256]{3,1,2,0:T(1,128)} collective-permute-done((f32[2,1,128,256]{3,1,2,0:T(1,128)S(1)}, f32[2,1,128,256]{3,1,2,0:T(1,128)}, u32[]{:S(2)}, u32[]{:S(2)}) %collective-permute-start.10) | collective-permute-done | bytes 262176 | tf_op jit(solution)/shard_map/ppermute | solution.py:282
  561.3 20.1 %collective-permute-done.13 = f32[2,1,128,256]{3,1,2,0:T(1,128)} collective-permute-done((f32[2,1,128,256]{3,1,2,0:T(1,128)S(1)}, f32[2,1,128,256]{3,1,2,0:T(1,128)}, u32[]{:S(2)}, u32[]{:S(2)}) %collective-permute-start.13) | collective-permute-done | bytes 262176 | tf_op jit(solution)/shard_map/ppermute | solution.py:282
  582.5 10.1 %collective-permute-done.14 = f32[2,1,128,256]{3,1,2,0:T(1,128)} collective-permute-done((f32[2,1,128,256]{3,1,2,0:T(1,128)S(1)}, f32[2,1,128,256]{3,1,2,0:T(1,128)}, u32[]{:S(2)}, u32[]{:S(2)}) %collective-permute-start.14) | collective-permute-done | bytes 262176 | tf_op jit(solution)/shard_map/ppermute | solution.py:282
  595.2 8.5 %collective-permute-done.15 = f32[2,1,128,256]{3,1,2,0:T(1,128)S(1)} collective-permute-done((f32[2,1,128,256]{3,1,2,0:T(1,128)S(1)}, f32[2,1,128,256]{3,1,2,0:T(1,128)S(1)}, u32[]{:S(2)}, u32[]{:S(2)}) %collective-permute-start.15) | collective-permute-done | bytes 262176 | tf_op jit(solution)/shard_map/ppermute | solution.py:282
  632.8 15.4 %convolution_bitcast_fusion = f32[2,32,2,128,256]{4,1,3,2,0:T(8,128)S(1)} fusion(f32[2,16,128,256,1,1]{3,1,0,2,5,4:T(8,128)} %copy.221, f32[1,2,2,32,16]{3,4,2,1,0:T(8,128)S(1)} %maximum_bitcast_fusion.45, f32[1,2,2,32,16]{3,4,2,1,0:T(8,128)S(1)} %copy-done.28), kind=kOutput, calls=%fused_computation.32 | convolution fusion | flops 1610616832 | bytes 20987904 | tf_op jit(solution)/shard_map/oafem,emRj->oafRj/dot_general | solution.py:147
  653.5 6.9 fusion.37
  660.4 7.1 fusion.50
  670.7 8.1 %fusion.39 = f32[32,128,2,64,1]{1,3,4,2,0:T(8,128)S(1)} fusion(f32[32,2,128,128,1]{3,0,2,1,4:T(8,128)} %copy-done.6, f32[2,2,128,2,64]{2,4,1,3,0:T(8,128)S(1)} %fusion.74), kind=kOutput, calls=%fused_computation.82 | convolution fusion | flops 1610612736 | bytes 6422528 | tf_op jit(solution)/shard_map/aeRu,eufk->aRfk/dot_general | solution.py:165
  678.8 6.9 fusion.51
  686.9 29.4 %collective-permute-done.20 = f32[2,128,2048]{1,2,0:T(8,128)} collective-permute-done((f32[2,128,2048]{1,2,0:T(8,128)S(1)}, f32[2,128,2048]{1,2,0:T(8,128)}, u32[]{:S(2)}, u32[]{:S(2)}) %collective-permute-start.20) | collective-permute-done | bytes 2097184 | tf_op jit(solution)/shard_map/ppermute | solution.py:292
  (326 shorter events, 252.3 us)
Async XLA Ops:
  0.0 143.1 %copy-start = (f32[4,2]{0,1:T(2,128)S(1)}, f32[4,2]{0,1:T(2,128)}, u32[]{:S(2)}) copy-start(f32[4,2]{0,1:T(2,128)} %param.23) | copy-start | bytes 100
  39.2 98.6 %all-to-all-start.1 = ((f32[16,2,128,256]{2,3,1,0:T(8,128)}), f32[16,2,128,256]{2,3,1,0:T(8,128)}, u32[]{:S(2)}, u32[]{:S(2)}) async-start(f32[16,2,128,256]{2,3,1,0:T(8,128)} %scatter.4), calls=%async_computation.1 | async-start | bytes 8388608 | tf_op jit(solution)/shard_map/all_to_all | solution.py:207
  45.5 47.6 %copy-start.41 = (pred[128]{0:T(512)(128)(4,1)}, pred[128]{0:T(512)(128)(4,1)S(1)}, u32[]{:S(2)}) copy-start(pred[128]{0:T(512)(128)(4,1)S(1)} %get-tuple-element.260) | copy-start | bytes 388
  105.7 37.1 %copy-start.13 = (f32[2,32,128]{2,1,0:T(8,128)S(1)}, f32[2,32,128]{2,1,0:T(8,128)}, u32[]{:S(2)}) copy-start(f32[2,32,128]{2,1,0:T(8,128)} %copy-done.12) | copy-start | bytes 98308
  105.7 37.2 %copy-start.11 = (f32[2,32,128]{2,1,0:T(8,128)S(1)}, f32[2,32,128]{2,1,0:T(8,128)}, u32[]{:S(2)}) copy-start(f32[2,32,128]{2,1,0:T(8,128)} %copy-done.10) | copy-start | bytes 98308
  137.8 229.8 %all-to-all-start = ((bf16[16,2,2,256,256]{3,4,2,1,0:T(8,128)(2,1)}), bf16[16,2,2,256,256]{3,4,2,1,0:T(8,128)(2,1)}, u32[]{:S(2)}, u32[]{:S(2)}) async-start(bf16[16,2,2,256,256]{3,4,2,1,0:T(8,128)(2,1)} %pad_maximum_fusion), calls=%async_computation | async-start | bytes 16777216 | tf_op jit(solution)/shard_map/all_to_all | solution.py:222
  148.5 92.9 %collective-permute-start = (f32[2,2048,256]{2,1,0:T(8,128)}, f32[2,2048,256]{2,1,0:T(8,128)}, u32[]{:S(2)}, u32[]{:S(2)}) collective-permute-start(f32[2,2048,256]{2,1,0:T(8,128)} %bitcast.589), channel_id=1, source_target_pairs={{0,16},{16,0},{1,17},{17,1},{2,18},{18,2},{3,19},{19,3},{4,20},{20... | collective-permute-start | bytes 12582920 | tf_op jit(solution)/shard_map/ppermute | solution.py:208
  405.8 34.0 %copy-start.2 = (f32[32,2,128,256]{3,0,2,1:T(8,128)}, f32[32,2,128,256]{3,0,2,1:T(8,128)S(1)}, u32[]{:S(2)}) copy-start(f32[32,2,128,256]{3,0,2,1:T(8,128)S(1)} %pad_maximum_fusion.2) | copy-start | bytes 25165828
  415.3 52.0 %collective-permute-start.1 = (f32[2,16,32,256]{3,1,2,0:T(8,128)S(1)}, f32[2,16,32,256]{3,1,2,0:T(8,128)S(1)}, u32[]{:S(2)}, u32[]{:S(2)}) collective-permute-start(f32[2,16,32,256]{3,1,2,0:T(8,128)S(1)} %fusion.56), channel_id=1, source_target_pairs={{0,16},{16,0},{1,17},{17,1},{2,18},{18,2},{3,19},{19,3},{4,20},{20... | collective-permute-start | bytes 3145736 | tf_op jit(solution)/shard_map/ppermute | solution.py:260
  427.3 40.0 %collective-permute-start.2 = (f32[2,16,32,256]{3,1,2,0:T(8,128)}, f32[2,16,32,256]{3,1,2,0:T(8,128)S(1)}, u32[]{:S(2)}, u32[]{:S(2)}) collective-permute-start(f32[2,16,32,256]{3,1,2,0:T(8,128)} %fusion.59), channel_id=1, source_target_pairs={{0,16},{16,0},{1,17},{17,1},{2,18},{18,2},{3,19},{19,3},{4,20},{20... | collective-permute-start | bytes 3145736 | tf_op jit(solution)/shard_map/ppermute | solution.py:260
  427.8 12.0 %copy-start.33 = (f32[1,2,16,128]{3,2,1,0:T(8,128)S(1)}, f32[1,2,16,128]{3,2,1,0:T(8,128)}, u32[]{:S(2)}) copy-start(f32[1,2,16,128]{3,2,1,0:T(8,128)} %get-tuple-element.199) | copy-start | bytes 49156
  427.8 12.0 %copy-start.34 = (f32[1,2,16,128]{3,2,1,0:T(8,128)S(1)}, f32[1,2,16,128]{3,2,1,0:T(8,128)}, u32[]{:S(2)}) copy-start(f32[1,2,16,128]{3,2,1,0:T(8,128)} %get-tuple-element.200) | copy-start | bytes 49156
  438.4 48.1 %collective-permute-start.3 = (f32[2,16,32,256]{3,1,2,0:T(8,128)}, f32[2,16,32,256]{3,1,2,0:T(8,128)}, u32[]{:S(2)}, u32[]{:S(2)}) collective-permute-start(f32[2,16,32,256]{3,1,2,0:T(8,128)} %fusion.62), channel_id=1, source_target_pairs={{0,16},{16,0},{1,17},{17,1},{2,18},{18,2},{3,19},{19,3},{4,20},{20... | collective-permute-start | bytes 3145736 | tf_op jit(solution)/shard_map/ppermute | solution.py:260
  439.9 11.6 %copy-start.20 = (f32[1,2,64,128]{3,2,1,0:T(8,128)S(1)}, f32[1,2,64,128]{3,2,1,0:T(8,128)}, u32[]{:S(2)}) copy-start(f32[1,2,64,128]{3,2,1,0:T(8,128)} %get-tuple-element.270) | copy-start | bytes 196612
  450.7 56.5 %collective-permute-start.4 = (f32[2,16,32,256]{3,1,2,0:T(8,128)}, f32[2,16,32,256]{3,1,2,0:T(8,128)}, u32[]{:S(2)}, u32[]{:S(2)}) collective-permute-start(f32[2,16,32,256]{3,1,2,0:T(8,128)} %fusion.65), channel_id=1, source_target_pairs={{0,16},{16,0},{1,17},{17,1},{2,18},{18,2},{3,19},{19,3},{4,20},{20... | collective-permute-start | bytes 3145736 | tf_op jit(solution)/shard_map/ppermute | solution.py:260
  518.3 8.2 %collective-permute-start.5 = (f32[2,1,128,256]{3,1,2,0:T(1,128)}, f32[2,1,128,256]{3,1,2,0:T(1,128)}, u32[]{:S(2)}, u32[]{:S(2)}) collective-permute-start(f32[2,1,128,256]{3,1,2,0:T(1,128)} %get-tuple-element.165), channel_id=1, source_target_pairs={{0,1},{1,0},{2,3},{3,2},{4,5},{5,4},{6,7},{7,6},{8,9},{9,8},{10,11... | collective-permute-start | bytes 786440 | tf_op jit(solution)/shard_map/ppermute | solution.py:282
  518.3 9.9 %collective-permute-start.6 = (f32[2,1,128,256]{3,1,2,0:T(1,128)}, f32[2,1,128,256]{3,1,2,0:T(1,128)}, u32[]{:S(2)}, u32[]{:S(2)}) collective-permute-start(f32[2,1,128,256]{3,1,2,0:T(1,128)} %get-tuple-element.164), channel_id=1, source_target_pairs={{0,2},{1,3},{2,0},{3,1},{4,6},{5,7},{6,4},{7,5},{8,10},{9,11},{10,... | collective-permute-start | bytes 786440 | tf_op jit(solution)/shard_map/ppermute | solution.py:282
  519.1 14.0 %collective-permute-start.7 = (f32[2,1,128,256]{3,1,2,0:T(1,128)}, f32[2,1,128,256]{3,1,2,0:T(1,128)}, u32[]{:S(2)}, u32[]{:S(2)}) collective-permute-start(f32[2,1,128,256]{3,1,2,0:T(1,128)} %get-tuple-element.163), channel_id=1, source_target_pairs={{0,3},{1,2},{2,1},{3,0},{4,7},{5,6},{6,5},{7,4},{8,11},{9,10},{10,... | collective-permute-start | bytes 786440 | tf_op jit(solution)/shard_map/ppermute | solution.py:282
  520.4 16.1 %collective-permute-start.8 = (f32[2,1,128,256]{3,1,2,0:T(1,128)}, f32[2,1,128,256]{3,1,2,0:T(1,128)}, u32[]{:S(2)}, u32[]{:S(2)}) collective-permute-start(f32[2,1,128,256]{3,1,2,0:T(1,128)} %get-tuple-element.162), channel_id=1, source_target_pairs={{0,4},{1,5},{2,6},{3,7},{4,0},{5,1},{6,2},{7,3},{8,12},{9,13},{10,... | collective-permute-start | bytes 786440 | tf_op jit(solution)/shard_map/ppermute | solution.py:282
  521.0 18.3 %collective-permute-start.9 = (f32[2,1,128,256]{3,1,2,0:T(1,128)}, f32[2,1,128,256]{3,1,2,0:T(1,128)}, u32[]{:S(2)}, u32[]{:S(2)}) collective-permute-start(f32[2,1,128,256]{3,1,2,0:T(1,128)} %get-tuple-element.161), channel_id=1, source_target_pairs={{0,5},{1,4},{2,7},{3,6},{4,1},{5,0},{6,3},{7,2},{8,13},{9,12},{10,... | collective-permute-start | bytes 786440 | tf_op jit(solution)/shard_map/ppermute | solution.py:282
  526.5 23.6 %collective-permute-start.10 = (f32[2,1,128,256]{3,1,2,0:T(1,128)S(1)}, f32[2,1,128,256]{3,1,2,0:T(1,128)}, u32[]{:S(2)}, u32[]{:S(2)}) collective-permute-start(f32[2,1,128,256]{3,1,2,0:T(1,128)S(1)} %get-tuple-element.160), channel_id=1, source_target_pairs={{0,6},{1,7},{2,4},{3,5},{4,2},{5,3},{6,0},{7,1},{8,14},{9,15},{10,... | collective-permute-start | bytes 786440 | tf_op jit(solution)/shard_map/ppermute | solution.py:282
  528.2 26.9 %collective-permute-start.11 = (f32[2,1,128,256]{3,1,2,0:T(1,128)S(1)}, f32[2,1,128,256]{3,1,2,0:T(1,128)}, u32[]{:S(2)}, u32[]{:S(2)}) collective-permute-start(f32[2,1,128,256]{3,1,2,0:T(1,128)S(1)} %get-tuple-element.159), channel_id=1, source_target_pairs={{0,7},{1,6},{2,5},{3,4},{4,3},{5,2},{6,1},{7,0},{8,15},{9,14},{10,... | collective-permute-start | bytes 786440 | tf_op jit(solution)/shard_map/ppermute | solution.py:282
  533.0 24.1 %collective-permute-start.12 = (f32[2,1,128,256]{3,1,2,0:T(1,128)S(1)}, f32[2,1,128,256]{3,1,2,0:T(1,128)}, u32[]{:S(2)}, u32[]{:S(2)}) collective-permute-start(f32[2,1,128,256]{3,1,2,0:T(1,128)S(1)} %get-tuple-element.158), channel_id=1, source_target_pairs={{0,8},{1,9},{2,10},{3,11},{4,12},{5,13},{6,14},{7,15},{8,0},{9,1},... | collective-permute-start | bytes 786440 | tf_op jit(solution)/shard_map/ppermute | solution.py:282
  536.5 44.9 %collective-permute-start.13 = (f32[2,1,128,256]{3,1,2,0:T(1,128)S(1)}, f32[2,1,128,256]{3,1,2,0:T(1,128)}, u32[]{:S(2)}, u32[]{:S(2)}) collective-permute-start(f32[2,1,128,256]{3,1,2,0:T(1,128)S(1)} %get-tuple-element.157), channel_id=1, source_target_pairs={{0,9},{1,8},{2,11},{3,10},{4,13},{5,12},{6,15},{7,14},{8,1},{9,0},... | collective-permute-start | bytes 786440 | tf_op jit(solution)/shard_map/ppermute | solution.py:282
  539.3 53.4 %collective-permute-start.14 = (f32[2,1,128,256]{3,1,2,0:T(1,128)S(1)}, f32[2,1,128,256]{3,1,2,0:T(1,128)}, u32[]{:S(2)}, u32[]{:S(2)}) collective-permute-start(f32[2,1,128,256]{3,1,2,0:T(1,128)S(1)} %get-tuple-element.156), channel_id=1, source_target_pairs={{0,10},{1,11},{2,8},{3,9},{4,14},{5,15},{6,12},{7,13},{8,2},{9,3},... | collective-permute-start | bytes 786440 | tf_op jit(solution)/shard_map/ppermute | solution.py:282
  550.1 53.6 %collective-permute-start.15 = (f32[2,1,128,256]{3,1,2,0:T(1,128)S(1)}, f32[2,1,128,256]{3,1,2,0:T(1,128)S(1)}, u32[]{:S(2)}, u32[]{:S(2)}) collective-permute-start(f32[2,1,128,256]{3,1,2,0:T(1,128)S(1)} %get-tuple-element.155), channel_id=1, source_target_pairs={{0,11},{1,10},{2,9},{3,8},{4,15},{5,14},{6,13},{7,12},{8,3},{9,2},... | collective-permute-start | bytes 786440 | tf_op jit(solution)/shard_map/ppermute | solution.py:282
  555.1 54.5 %collective-permute-start.16 = (f32[2,1,128,256]{3,1,2,0:T(1,128)S(1)}, f32[2,1,128,256]{3,1,2,0:T(1,128)S(1)}, u32[]{:S(2)}, u32[]{:S(2)}) collective-permute-start(f32[2,1,128,256]{3,1,2,0:T(1,128)S(1)} %get-tuple-element.154), channel_id=1, source_target_pairs={{0,12},{1,13},{2,14},{3,15},{4,8},{5,9},{6,10},{7,11},{8,4},{9,5},... | collective-permute-start | bytes 786440 | tf_op jit(solution)/shard_map/ppermute | solution.py:282
  557.2 58.0 %collective-permute-start.17 = (f32[2,1,128,256]{3,1,2,0:T(1,128)S(1)}, f32[2,1,128,256]{3,1,2,0:T(1,128)S(1)}, u32[]{:S(2)}, u32[]{:S(2)}) collective-permute-start(f32[2,1,128,256]{3,1,2,0:T(1,128)S(1)} %get-tuple-element.153), channel_id=1, source_target_pairs={{0,13},{1,12},{2,15},{3,14},{4,9},{5,8},{6,11},{7,10},{8,5},{9,4},... | collective-permute-start | bytes 786440 | tf_op jit(solution)/shard_map/ppermute | solution.py:282
  581.4 39.5 %collective-permute-start.18 = (f32[2,1,128,256]{3,1,2,0:T(1,128)S(1)}, f32[2,1,128,256]{3,1,2,0:T(1,128)S(1)}, u32[]{:S(2)}, u32[]{:S(2)}) collective-permute-start(f32[2,1,128,256]{3,1,2,0:T(1,128)S(1)} %get-tuple-element.152), channel_id=1, source_target_pairs={{0,14},{1,15},{2,12},{3,13},{4,10},{5,11},{6,8},{7,9},{8,6},{9,7},... | collective-permute-start | bytes 786440 | tf_op jit(solution)/shard_map/ppermute | solution.py:282
  592.7 33.1 %collective-permute-start.19 = (f32[2,1,128,256]{3,1,2,0:T(1,128)S(1)}, f32[2,1,128,256]{3,1,2,0:T(1,128)S(1)}, u32[]{:S(2)}, u32[]{:S(2)}) collective-permute-start(f32[2,1,128,256]{3,1,2,0:T(1,128)S(1)} %get-tuple-element.151), channel_id=1, source_target_pairs={{0,15},{1,14},{2,13},{3,12},{4,11},{5,10},{6,9},{7,8},{8,7},{9,6},... | collective-permute-start | bytes 786440 | tf_op jit(solution)/shard_map/ppermute | solution.py:282
  653.5 14.0 %copy-start.6 = (f32[32,2,128,128,1]{3,0,2,1,4:T(8,128)}, f32[32,2,128,128,1]{3,0,2,1,4:T(8,128)S(1)}, u32[]{:S(2)}) copy-start(f32[32,2,128,128,1]{3,0,2,1,4:T(8,128)S(1)} %maximum_bitcast_fusion.5) | copy-start | bytes 12582916
  668.7 47.7 %collective-permute-start.20 = (f32[2,128,2048]{1,2,0:T(8,128)S(1)}, f32[2,128,2048]{1,2,0:T(8,128)}, u32[]{:S(2)}, u32[]{:S(2)}) collective-permute-start(f32[2,128,2048]{1,2,0:T(8,128)S(1)} %bitcast.590), channel_id=1, source_target_pairs={{0,16},{16,0},{1,17},{17,1},{2,18},{18,2},{3,19},{19,3},{4,20},{20... | collective-permute-start | bytes 6291464 | tf_op jit(solution)/shard_map/ppermute | solution.py:292
  (36 other events, 211.7 us)
